TPU v7x, 128 devices: a whole 4x4x4 slice. The times are simulated.
128 devices in a mesh: space: 32 (over x, z, core), feat: 4 (over y).
Axes of the slice: x: 4, y: 4, z: 4, core: 2. Of those that a mesh axis runs over, the one named last changes fastest.
Arguments:
- inputs: bfloat16 [2, 96, 180, 1024], P(None, 'space', None, 'feat'), may hold values from -15 to 15
- cotangent: bfloat16 [2, 96, 180, 1024], P(None, 'space', None, 'feat'), may hold values from -6 to 6
- spec_w1: float32 [2, 8, 128, 128], P(None, 'feat'), may hold values from -0.375 to 0.375
- spec_b1: float32 [2, 1024], P(None, 'feat'), may hold values from -0.3 to 0.3
- spec_w2: float32 [2, 8, 128, 128], P(None, 'feat'), may hold values from -0.375 to 0.375
- spec_b2: float32 [2, 1024], P(None, 'feat'), may hold values from -0.3 to 0.3
- up_weight: bfloat16 [1024, 4096], P(None, 'feat'), may hold values from -0.1875 to 0.1875
- down_weight: bfloat16 [4096, 1024], P('feat'), may hold values from -0.09375 to 0.09375
Outputs:
- output: bfloat16 [2, 96, 180, 1024], P(None, 'space', None, 'feat')
- grad_input: bfloat16 [2, 96, 180, 1024], P(None, 'space', None, 'feat')
All inputs are finite; a program needn't handle non-finite values.
Results may differ from a plain program's by a relative error of at most 0.0102.
Values may be sent and summed in bfloat16 or wider, within the bound.
No kernel may reach another device: no remote copies, remote signals or barrier semaphores. Data moves between devices by JAX's collectives and lax.ppermute only.
A program may use at most 128 MiB of HBM per device.

v0:
```python
import math
import jax
import jax.numpy as jnp
from jax import lax
from jax.sharding import PartitionSpec as P

EPSILON = 1e-05
SHRINK_LEVEL = 0.1
HIGHEST = lax.Precision.HIGHEST


def longitude_tables(width_lon):
    mode_count = width_lon // 2 + 1
    cell_index = jnp.arange(width_lon, dtype=jnp.int32)[:, None]
    wave_number = jnp.arange(mode_count, dtype=jnp.int32)[None, :]
    phase_angle = (
        2.0 * math.pi / width_lon * (cell_index * wave_number % width_lon).astype(jnp.float32)
    )
    scaling = 1.0 / math.sqrt(width_lon)
    cos_fwd = jnp.cos(phase_angle) * scaling
    sin_fwd = -jnp.sin(phase_angle) * scaling
    doubled = jnp.where((wave_number == 0) | (wave_number * 2 == width_lon), 1.0, 2.0).astype(
        jnp.float32
    )
    return (cos_fwd, sin_fwd, cos_fwd * doubled, sin_fwd * doubled)


def padded_tables(width_lon, multiple):
    tables = longitude_tables(width_lon)
    modes = tables[0].shape[1]
    extra = -modes % multiple
    return tuple((jnp.pad(table, ((0, 0), (0, extra))) for table in tables))


def lat_apply(table, field):
    return jnp.einsum("gh,bhkc->bgkc", table, field, precision=HIGHEST)


def complex_latitude(table_cos, table_sin, real_part, imag_part, inverse):
    if inverse:
        return (
            lat_apply(table_cos, real_part) + lat_apply(table_sin, imag_part),
            lat_apply(table_cos, imag_part) - lat_apply(table_sin, real_part),
        )
    return (
        lat_apply(table_cos, real_part) - lat_apply(table_sin, imag_part),
        lat_apply(table_cos, imag_part) + lat_apply(table_sin, real_part),
    )


def lon_forward(field, table):
    return jnp.einsum("brwc,wk->brkc", field, table, precision=HIGHEST)


def lon_back(spec, table):
    return jnp.einsum("brkc,wk->brwc", spec, table, precision=HIGHEST)


def to_blocks(field, block_size):
    return field.reshape(field.shape[:-1] + (field.shape[-1] // block_size, block_size))


def block_mult(field, weights):
    return jnp.einsum("...nc,nce->...ne", field, weights, precision=HIGHEST)


def block_mult_back(field, weights):
    return jnp.einsum("...ne,nce->...nc", field, weights, precision=HIGHEST)


def block_product(real_part, imag_part, weights):
    return (
        block_mult(real_part, weights[0]) - block_mult(imag_part, weights[1]),
        block_mult(real_part, weights[1]) + block_mult(imag_part, weights[0]),
    )


def block_adjoint(real_part, imag_part, weights):
    return (
        block_mult_back(real_part, weights[0]) + block_mult_back(imag_part, weights[1]),
        block_mult_back(imag_part, weights[0]) - block_mult_back(real_part, weights[1]),
    )


def latitude_tables(length):
    index_row = jnp.arange(length, dtype=jnp.int32)
    phase_angle = (
        2.0
        * math.pi
        / length
        * (index_row[:, None] * index_row[None, :] % length).astype(jnp.float32)
    )
    scaling = 1.0 / math.sqrt(length)
    return (jnp.cos(phase_angle) * scaling, -jnp.sin(phase_angle) * scaling)


def to_columns(real_part, imag_part, link_type):
    stacked = jnp.stack([real_part, imag_part]).astype(link_type)
    moved = lax.all_to_all(stacked, "space", 3, 2, tiled=True).astype(jnp.float32)
    return (moved[0], moved[1])


def to_rows(real_part, imag_part, link_type):
    stacked = jnp.stack([real_part, imag_part]).astype(link_type)
    moved = lax.all_to_all(stacked, "space", 2, 3, tiled=True).astype(jnp.float32)
    return (moved[0], moved[1])


def enter_spectrum(real_part, imag_part, tables_lat, link_type=jnp.float32):
    table_cos, table_sin = tables_lat
    real_part, imag_part = to_columns(real_part, imag_part, link_type)
    return complex_latitude(table_cos, table_sin, real_part, imag_part, False)


def leave_spectrum(real_part, imag_part, tables_lat, link_type=jnp.float32):
    table_cos, table_sin = tables_lat
    real_part, imag_part = complex_latitude(table_cos, table_sin, real_part, imag_part, True)
    return to_rows(real_part, imag_part, link_type)


def complex_operator(real_block, imag_block):
    return jnp.stack([jnp.stack([real_block, -imag_block]), jnp.stack([imag_block, real_block])])


def lat_stacked(operator, field, precision=lax.Precision.HIGH):
    return jnp.einsum("pqkh,qbhlc->pbklc", operator, field, precision=precision)


def lon_stacked_forward(field, tables, precision=lax.Precision.HIGH):
    return jnp.einsum("brwc,pwk->pbrkc", field, tables, precision=precision)


def lon_stacked_back(spec, tables, precision=lax.Precision.HIGH):
    return jnp.einsum("pbrkc,pwk->brwc", spec, tables, precision=precision)


def block_operator(weights):
    return jnp.moveaxis(complex_operator(weights[0], weights[1]), 2, 0)


def block_stacked(field, operator):
    return jnp.einsum("qbklnc,npqce->pbklne", field, operator, precision=lax.Precision.HIGH)


def block_stacked_adjoint(field, operator):
    return jnp.einsum("pbklne,npqce->qbklnc", field, operator, precision=lax.Precision.DEFAULT)


def stacked_columns(field, link_type):
    return lax.all_to_all(field.astype(link_type), "space", 3, 2, tiled=True).astype(jnp.float32)


def stacked_rows(field, link_type):
    return lax.all_to_all(field.astype(link_type), "space", 2, 3, tiled=True).astype(jnp.float32)


def token_sums(first_term, second_term):
    pair = jnp.stack([first_term, second_term])
    count = lax.axis_size("feat")
    shifted = jnp.stack(
        [pair]
        + [
            lax.ppermute(pair, "feat", [(i, (i + count - shift) % count) for i in range(count)])
            for shift in range(1, count)
        ]
    )
    total = shifted[0]
    for source in range(1, count):
        total = total + shifted[source]
    return (total[0], total[1])


def ring_send(block):
    count = lax.axis_size("feat")
    return [block] + [
        lax.ppermute(block, "feat", [(i, (i + shift) % count) for i in range(count)])
        for shift in range(1, count)
    ]


def ring_assemble(parts):
    count = len(parts)
    position = lax.axis_index("feat")
    block = parts[0]
    width = block.shape[-1]
    whole = jnp.zeros(block.shape[:-1] + (width * count,), block.dtype)
    for shift, moved in enumerate(parts):
        source = (position + count - shift) % count
        whole = lax.dynamic_update_slice_in_dim(whole, moved, source * width, axis=block.ndim - 1)
    return whole


def channel_share(term):
    return lax.psum_scatter(
        term.astype(jnp.bfloat16), "feat", scatter_dimension=3, tiled=True
    ).astype(jnp.float32)


def gelu_value(field):
    return 0.5 * field * (1.0 + lax.erf(field * (1.0 / math.sqrt(2.0))))


def gelu_slope(field):
    return 0.5 * (1.0 + lax.erf(field * (1.0 / math.sqrt(2.0)))) + field * jnp.exp(
        -0.5 * field * field
    ) * (1.0 / math.sqrt(2.0 * math.pi))


def per_device(inputs, cotangent, spec_w1, spec_b1, spec_w2, spec_b2, up_weight, down_weight):
    full_width = up_weight.shape[0]
    block_size = spec_w1.shape[2]
    tables_lon = padded_tables(inputs.shape[2], lax.axis_size("space"))
    tables_lat = latitude_tables(inputs.shape[1] * lax.axis_size("space"))
    cos_fwd, sin_fwd, cos_inv, sin_inv = tables_lon
    table_cos, table_sin = tables_lat
    operators = (
        jnp.stack([cos_fwd, sin_fwd]),
        jnp.stack([cos_inv, sin_inv]),
        complex_operator(table_cos, table_sin),
        complex_operator(table_cos, -table_sin),
        block_operator(spec_w1),
        block_operator(spec_w2),
    )
    operators = lax.optimization_barrier(operators)
    lon_fwd_tables, lon_inv_tables, lat_forward_op, lat_inverse_op, first_op, second_op = operators
    values = inputs.astype(jnp.float32)
    cotangent_parts = lax.all_gather(cotangent, "feat", axis=3, tiled=True)
    first_sum, second_sum = token_sums(jnp.sum(values, axis=-1), jnp.sum(values * values, axis=-1))
    mean_one = first_sum[..., None] / full_width
    rstd_one = lax.rsqrt(second_sum[..., None] / full_width - mean_one * mean_one + EPSILON)
    normed = (values - mean_one) * rstd_one
    spec = lat_stacked(
        lat_forward_op, stacked_columns(lon_stacked_forward(normed, lon_fwd_tables), jnp.float32)
    )
    spec_blocks = to_blocks(spec, block_size)
    bias_one = to_blocks(spec_b1, block_size)[:, None, None, None]
    bias_two = to_blocks(spec_b2, block_size)[:, None, None, None]
    first = jax.nn.relu(block_stacked(spec_blocks, first_op) + bias_one)
    second = block_stacked(first, second_op) + bias_two
    shrunk = (second - jnp.clip(second, -SHRINK_LEVEL, SHRINK_LEVEL)).reshape(spec.shape)
    shrunk, cotangent_parts = lax.optimization_barrier((shrunk, cotangent_parts))
    whole_cotangent = cotangent_parts
    filtered = lon_stacked_back(
        stacked_rows(lat_stacked(lat_inverse_op, shrunk, lax.Precision.DEFAULT), jnp.bfloat16),
        lon_inv_tables,
        lax.Precision.DEFAULT,
    )
    residual = (filtered + normed + values).astype(jnp.bfloat16)
    residual_vals = residual.astype(jnp.float32)
    whole_residual = lax.all_gather(residual, "feat", axis=3, tiled=True)
    grad_act = jnp.einsum(
        "brwd,hd->brwh", whole_cotangent, down_weight, preferred_element_type=jnp.float32
    )
    whole_residual, grad_act = lax.optimization_barrier((whole_residual, grad_act))
    whole_vals = whole_residual.astype(jnp.float32)
    mean_two = jnp.sum(whole_vals, axis=-1, keepdims=True) / full_width
    square_two = jnp.sum(whole_vals * whole_vals, axis=-1, keepdims=True) / full_width
    rstd_two = lax.rsqrt(square_two - mean_two * mean_two + EPSILON)
    vhat = (whole_vals - mean_two) * rstd_two
    hidden = jnp.einsum(
        "brwd,dh->brwh", vhat.astype(jnp.bfloat16), up_weight, preferred_element_type=jnp.float32
    )
    activated = gelu_value(hidden).astype(jnp.bfloat16)
    mixed_term = jnp.einsum(
        "brwh,hd->brwd", activated, down_weight, preferred_element_type=jnp.float32
    )
    output = (residual_vals + channel_share(mixed_term)).astype(jnp.bfloat16)
    grad_hidden = (grad_act * gelu_slope(hidden)).astype(jnp.bfloat16)
    grad_term = jnp.einsum(
        "brwh,dh->brwd", grad_hidden, up_weight, preferred_element_type=jnp.float32
    )
    total_one, total_two = token_sums(
        jnp.sum(grad_term, axis=-1), jnp.sum(grad_term * vhat, axis=-1)
    )
    grad_vhat = channel_share(grad_term)
    own_hat = (residual_vals - mean_two) * rstd_two
    grad_residual = cotangent.astype(jnp.float32) + rstd_two * (
        grad_vhat
        - total_one[..., None] / full_width
        - own_hat * (total_two[..., None] / full_width)
    )
    grad_spec = lat_stacked(
        lat_forward_op,
        stacked_columns(
            lon_stacked_forward(grad_residual, lon_inv_tables, lax.Precision.DEFAULT), jnp.bfloat16
        ),
        lax.Precision.DEFAULT,
    )
    grad_second = jnp.where(jnp.abs(second) > SHRINK_LEVEL, to_blocks(grad_spec, block_size), 0.0)
    grad_first = jnp.where(first > 0.0, block_stacked_adjoint(grad_second, second_op), 0.0)
    grad_spectrum = block_stacked_adjoint(grad_first, first_op).reshape(spec.shape)
    grad_normed = grad_residual + lon_stacked_back(
        stacked_rows(
            lat_stacked(lat_inverse_op, grad_spectrum, lax.Precision.DEFAULT), jnp.bfloat16
        ),
        lon_fwd_tables,
        lax.Precision.DEFAULT,
    )
    norm_one, norm_two = token_sums(
        jnp.sum(grad_normed, axis=-1), jnp.sum(grad_normed * normed, axis=-1)
    )
    grad_input = grad_residual + rstd_one * (
        grad_normed - norm_one[..., None] / full_width - normed * (norm_two[..., None] / full_width)
    )
    return (output, grad_input.astype(jnp.bfloat16))


def solution(mesh):
    return jax.shard_map(
        per_device,
        mesh=mesh,
        in_specs=(
            P(None, "space", None, "feat"),
            P(None, "space", None, "feat"),
            P(None, "feat", None, None),
            P(None, "feat"),
            P(None, "feat", None, None),
            P(None, "feat"),
            P(None, "feat"),
            P("feat", None),
        ),
        out_specs=(P(None, "space", None, "feat"), P(None, "space", None, "feat")),
        check_vma=False,
    )
```

profile of v0, /device:TPU:1, one launch (start us, length us, event | category | flops | bytes accessed | tf_op | source)
XLA Modules:
  0.0 219.6 jit_solution(13806531281613694137)
XLA Ops:
  7.2 1.7 convert_reduce_fusion.1
  9.0 3.8 %collective-permute-start.1 = (f32[2,2,3,180]{3,2,1,0:T(4,128)S(1)}, f32[2,2,3,180]{3,2,1,0:T(4,128)S(1)}, u32[]{:S(2)}, u32[]{:S(2)}) collective-permute-start(f32[2,2,3,180]{3,2,1,0:T(4,128)S(1)} %pad_maximum_fusion.8), channel_id=1, source_target_pairs={{0,2},{1,3},{2,0},{3,1},{4,6},{5,7},{6,4},{7,5},{8,10},{9,11},{10,... | collective-permute-start | bytes 25928 | tf_op jit(solution)/shard_map/ppermute | solution.py:163
  13.2 2.3 %collective-permute-start = (f32[2,2,3,180]{3,2,1,0:T(4,128)S(1)}, f32[2,2,3,180]{3,2,1,0:T(4,128)S(1)}, u32[]{:S(2)}, u32[]{:S(2)}) collective-permute-start(f32[2,2,3,180]{3,2,1,0:T(4,128)S(1)} %pad_maximum_fusion.8), channel_id=1, source_target_pairs={{0,3},{1,0},{2,1},{3,2},{4,7},{5,4},{6,5},{7,6},{8,11},{9,8},{10,9... | collective-permute-start | bytes 25928 | tf_op jit(solution)/shard_map/ppermute | solution.py:163
  16.8 0.4 fusion.97
  17.4 0.7 pad_maximum_fusion.1
  18.2 1.1 maximum_bitcast_fusion.1
  19.3 0.7 pad_maximum_fusion.3
  20.1 1.0 convolution_bitcast_fusion.7
  21.1 0.9 copy.96
  22.0 28.2 %all_to_all.72 = f32[2,2,3,96,256]{4,1,2,0,3:T(2,128)S(1)} all-to-all(f32[2,2,3,96,256]{4,1,2,0,3:T(2,128)S(1)} %copy.96), channel_id=1, replica_groups=mesh['space'=32,'feat'=4] {'space'}, dimensions={3} | all-to-all | bytes 2359296 | tf_op jit(solution)/shard_map/all_to_all | solution.py:150
  50.6 0.7 convolution_bitcast_fusion.6
  51.3 1.6 reshape.195
  52.9 2.1 fusion.31
  55.1 0.7 fusion.32
  55.7 1.0 copy-done.1
  56.8 1.0 copy_bitcast_fusion
  57.7 1.4 fusion.42
  59.1 0.6 copy.108
  59.8 16.0 %all_to_all.73 = bf16[2,2,96,3,256]{4,0,3,1,2:T(2,128)(2,1)S(1)} all-to-all(bf16[2,2,96,3,256]{4,0,3,1,2:T(2,128)(2,1)S(1)} %copy.108), channel_id=1, replica_groups=mesh['space'=32,'feat'=4] {'space'}, dimensions={2} | all-to-all | bytes 1179648 | tf_op jit(solution)/shard_map/all_to_all | solution.py:154
  75.8 0.5 copy.110
  76.2 1.3 fusion.37
  77.6 6.9 %fusion.16 = f32[2,3,180,1024]{3,2,1,0:T(8,128)} fusion(bf16[2,3,180,1024]{3,0,2,1:T(2,128)(2,1)} %all-gather.3.cloned.1.call-done, bf16[1024,1024]{1,0:T(8,128)(2,1)} %param.15), kind=kOutput, calls=%fused_computation.20 | convolution fusion | flops 2264924160 | bytes 8732672 | tf_op jit(solution)/shard_map/brwd,hd->brwh/dot_general | solution.py:251
  84.5 23.0 %all-gather.5.cloned.1.call-done = bf16[2,3,180,1024]{3,2,1,0:T(8,128)(2,1)} async-done(((bf16[2,3,180,256]{3,2,1,0:T(8,128)(2,1)}), bf16[2,3,180,1024]{3,2,1,0:T(8,128)(2,1)}) %all-gather.5.cloned.1.call-update) | async-done | bytes 2211856 | tf_op jit(solution)/shard_map/all_gather | solution.py:250
  107.6 2.5 %convert_reduce_fusion = (f32[2,3,180]{2,1,0:T(4,128)S(1)}, f32[2,3,180]{2,1,0:T(4,128)S(1)}) fusion(bf16[2,3,180,1024]{3,2,1,0:T(8,128)(2,1)} %all-gather.5.cloned.1.call-done), kind=kLoop, calls=%fused_computation.3 | loop fusion | flops 4421520 | bytes 2220480 | tf_op jit(solution)/shard_map/reduce_sum | solution.py:256
  110.2 2.8 %fusion.14 = f32[2,3,180,1024]{3,2,1,0:T(8,128)S(1)} fusion(bf16[2,3,180,1024]{3,2,1,0:T(8,128)(2,1)S(1)} %copy-done.8, f32[2,3,180]{2,1,0:T(4,128)S(1)} %get-tuple-element.60, f32[2,3,180]{2,1,0:T(4,128)S(1)} %get-tuple-element.59, bf16[1024,1024]{1,0:T(8,128)(2,1)S(1)} %copy-done), kind=kOutput, calls=%fused_computation.19 | convolution fusion | flops 2269347840 | bytes 8741312 | tf_op jit(solution)/shard_map/brwd,dh->brwh/dot_general | solution.py:260
  113.1 5.4 %fusion.123 = (f32[2,3,180]{2,1,0:T(4,128)S(1)}, f32[2,3,180]{2,1,0:T(4,128)S(1)}, bf16[2,3,180,1024]{3,2,1,0:T(8,128)(2,1)}) fusion(f32[2,3,180]{2,1,0:T(4,128)S(1)} %get-tuple-element.60, f32[2,3,180]{2,1,0:T(4,128)S(1)} %get-tuple-element.59, bf16[2,3,180,1024]{3,2,1,0:T(8,128)(2,1)S(1)} %copy-done.8, bf16[1024,1024]{1,0:T(8,128)(2,1)S(1)} %copy-done, ...), kind=kOutput, calls=%fused_computation.189 | convolution fusion | flops 2283722752 | bytes 15385472 | tf_op jit(solution)/shard_map/brwh,dh->brwd/dot_general | solution.py:269
  118.5 6.9 %fusion.28 = bf16[2,3,180,1024]{3,2,1,0:T(8,128)(2,1)} fusion(bf16[1024,1024]{1,0:T(8,128)(2,1)} %param.15, f32[2,3,180,1024]{3,2,1,0:T(8,128)} %copy-done.19), kind=kOutput, calls=%fused_computation.36 | convolution fusion | flops 2271559680 | bytes 8732672 | tf_op jit(solution)/shard_map/brwh,hd->brwd/dot_general | solution.py:264
  125.5 2.5 %collective-permute-start.4 = (f32[2,2,3,180]{3,2,1,0:T(4,128)S(1)}, f32[2,2,3,180]{3,2,1,0:T(4,128)S(1)}, u32[]{:S(2)}, u32[]{:S(2)}) collective-permute-start(f32[2,2,3,180]{3,2,1,0:T(4,128)S(1)} %pad_maximum_fusion.9), channel_id=1, source_target_pairs={{0,2},{1,3},{2,0},{3,1},{4,6},{5,7},{6,4},{7,5},{8,10},{9,11},{10,... | collective-permute-start | bytes 25928 | tf_op jit(solution)/shard_map/ppermute | solution.py:163
  128.0 2.7 %collective-permute-start.3 = (f32[2,2,3,180]{3,2,1,0:T(4,128)S(1)}, f32[2,2,3,180]{3,2,1,0:T(4,128)S(1)}, u32[]{:S(2)}, u32[]{:S(2)}) collective-permute-start(f32[2,2,3,180]{3,2,1,0:T(4,128)S(1)} %pad_maximum_fusion.9), channel_id=1, source_target_pairs={{0,3},{1,0},{2,1},{3,2},{4,7},{5,4},{6,5},{7,6},{8,11},{9,8},{10,9... | collective-permute-start | bytes 25928 | tf_op jit(solution)/shard_map/ppermute | solution.py:163
  130.7 1.3 collective-permute-done.5
  132.0 19.8 %reduce-scatter.5.cloned.1.call-done = bf16[2,3,180,256]{3,2,1,0:T(8,128)(2,1)} async-done(((bf16[2,3,180,1024]{3,2,1,0:T(8,128)(2,1)}), bf16[2,3,180,256]{3,2,1,0:T(8,128)(2,1)}) %reduce-scatter.5.cloned.1.call-update) | async-done | bytes 552976 | tf_op jit(solution)/shard_map/reduce_scatter | solution.py:194
  151.8 2.3 %fusion.40 = bf16[2,2,3,96,256]{4,3,2,1,0:T(8,128)(2,1)S(1)} fusion(bf16[2,180,96]{2,1,0:T(8,128)(2,1)} %pad_maximum_fusion.3, bf16[2,3,180,256]{3,2,1,0:T(8,128)(2,1)} %fusion.37, bf16[2,3,180,256]{3,2,1,0:T(8,128)(2,1)} %reduce-scatter.5.cloned.1.call-done, bf16[2,3,180,256]{3,0,2,1:T(2,128)(2,1)} %param.9, f32[2,3,180]{2,1,0:T(4,128)S(1)} %get-tuple-element.58, ...), kind=kOutput, calls=%fused_computation.61 | convolution fusion | flops 108933120 | bytes 2335104 | tf_op jit(solution)/shard_map/brwc,pwk->pbrkc/dot_general | solution.py:130
  154.1 0.6 copy.114
  154.7 19.7 %all_to_all.74 = bf16[2,2,3,96,256]{4,1,2,0,3:T(2,128)(2,1)S(1)} all-to-all(bf16[2,2,3,96,256]{4,1,2,0,3:T(2,128)(2,1)S(1)} %copy.114), channel_id=1, replica_groups=mesh['space'=32,'feat'=4] {'space'}, dimensions={3} | all-to-all | bytes 1179648 | tf_op jit(solution)/shard_map/all_to_all | solution.py:150
  174.8 1.2 convolution_bitcast_fusion.8
  176.0 2.5 %reshape.229 = bf16[2,2,96,3,2,128]{5,4,2,0,3,1:T(2,128)(2,1)} reshape(bf16[2,2,96,3,256]{4,2,0,3,1:T(8,128)(2,1)} %convolution_bitcast_fusion.8) | data formatting | bytes 1179648 | tf_op jit(solution)/shard_map/reshape | solution.py:60
  178.5 2.1 fusion.39
  181.0 0.6 copy.189
  182.3 0.6 copy.126
  183.0 15.9 %all_to_all.75 = bf16[2,2,96,3,256]{4,0,3,1,2:T(2,128)(2,1)S(1)} all-to-all(bf16[2,2,96,3,256]{4,0,3,1,2:T(2,128)(2,1)S(1)} %copy.126), channel_id=1, replica_groups=mesh['space'=32,'feat'=4] {'space'}, dimensions={2} | all-to-all | bytes 1179648 | tf_op jit(solution)/shard_map/all_to_all | solution.py:154
  198.9 0.5 copy.128
  199.4 2.7 %fusion.124 = (f32[2,3,180]{2,1,0:T(4,128)S(1)}, f32[2,3,180]{2,1,0:T(4,128)S(1)}, f32[2,3,180,256]{3,2,1,0:T(8,128)}) fusion(f32[2,3,180]{2,1,0:T(4,128)S(1)} %fusion.115, f32[2,3,180]{2,1,0:T(4,128)S(1)} %fusion.116, bf16[2,3,180,256]{3,0,2,1:T(2,128)(2,1)S(1)} %copy-done.4, bf16[2,2,3,96,256]{4,1,3,2,0:T(2,128)(2,1)S(1)} %bitcast.284, ...), kind=kOutput, calls=%fused_computation.190 | convolution fusion | flops 110866320 | bytes 4080384 | tf_op jit(solution)/shard_map/pbrkc,pwk->brwc/dot_general | solution.py:134
  202.1 1.3 collective-permute-start.7
  203.4 2.6 %collective-permute-start.6 = (f32[2,2,3,180]{3,2,1,0:T(4,128)S(1)}, f32[2,2,3,180]{3,2,1,0:T(4,128)S(1)}, u32[]{:S(2)}, u32[]{:S(2)}) collective-permute-start(f32[2,2,3,180]{3,2,1,0:T(4,128)S(1)} %pad_maximum_fusion.10), channel_id=1, source_target_pairs={{0,3},{1,0},{2,1},{3,2},{4,7},{5,4},{6,5},{7,6},{8,11},{9,8},{10,9... | collective-permute-start | bytes 25928 | tf_op jit(solution)/shard_map/ppermute | solution.py:163
  206.3 0.9 collective-permute-done.8
  207.3 3.4 %fusion.68 = (bf16[2,3,180,256]{3,2,1,0:T(8,128)(2,1)S(1)}, bf16[2,3,180,256]{3,2,1,0:T(8,128)(2,1)S(1)}) fusion(f32[2,3,180,256]{3,2,1,0:T(8,128)} %get-tuple-element.64, f32[2,3,180]{2,1,0:T(4,128)S(1)} %get-tuple-element.56, f32[2,3,180]{2,1,0:T(4,128)S(1)} %get-tuple-element.55, f32[2,3,180]{2,1,0:T(4,128)S(1)} %fusion.115, ...), kind=kLoop, calls=%fused_computation.92 | loop fusion | flops 6082560 | bytes 5011200 | tf_op jit(solution)/shard_map/convert_element_type | solution.py:305
  210.6 1.2 copy.131
  211.9 1.2 copy.130
  (95 shorter events, 4.5 us)
Async XLA Ops:
  7.2 103.0 %copy-start = (bf16[1024,1024]{1,0:T(8,128)(2,1)S(1)}, bf16[1024,1024]{1,0:T(8,128)(2,1)}, u32[]{:S(2)}) copy-start(bf16[1024,1024]{1,0:T(8,128)(2,1)} %param.14) | copy-start | bytes 6291460
  7.2 10.1 %copy-start.14 = (f32[2,2,128,128]{3,2,1,0:T(8,128)S(1)}, f32[2,2,128,128]{3,2,1,0:T(8,128)}, u32[]{:S(2)}) copy-start(f32[2,2,128,128]{3,2,1,0:T(8,128)} %param.10) | copy-start | bytes 786436
  7.2 50.5 %all-gather.3.cloned.1.call-start = ((), (), s32[]{:S(2)}) async-start(), calls=%async_computation.6 | async-start | bytes 2764800 | tf_op jit(solution)/shard_map/all_gather | solution.py:227
  9.0 8.4 %copy-start.15 = (f32[2,2,128,128]{3,2,1,0:T(8,128)S(1)}, f32[2,2,128,128]{3,2,1,0:T(8,128)}, u32[]{:S(2)}) copy-start(f32[2,2,128,128]{3,2,1,0:T(8,128)} %param.12) | copy-start | bytes 786436
  9.0 11.0 %collective-permute-start.1 = (f32[2,2,3,180]{3,2,1,0:T(4,128)S(1)}, f32[2,2,3,180]{3,2,1,0:T(4,128)S(1)}, u32[]{:S(2)}, u32[]{:S(2)}) collective-permute-start(f32[2,2,3,180]{3,2,1,0:T(4,128)S(1)} %pad_maximum_fusion.8), channel_id=1, source_target_pairs={{0,2},{1,3},{2,0},{3,1},{4,6},{5,7},{6,4},{7,5},{8,10},{9,11},{10,... | collective-permute-start | bytes 25928 | tf_op jit(solution)/shard_map/ppermute | solution.py:163
  12.8 7.2 %collective-permute-start.2 = (f32[2,2,3,180]{3,2,1,0:T(4,128)S(1)}, f32[2,2,3,180]{3,2,1,0:T(4,128)S(1)}, u32[]{:S(2)}, u32[]{:S(2)}) collective-permute-start(f32[2,2,3,180]{3,2,1,0:T(4,128)S(1)} %pad_maximum_fusion.8), channel_id=1, source_target_pairs={{0,1},{1,2},{2,3},{3,0},{4,5},{5,6},{6,7},{7,4},{8,9},{9,10},{10,1... | collective-permute-start | bytes 25928 | tf_op jit(solution)/shard_map/ppermute | solution.py:163
  13.2 6.8 %collective-permute-start = (f32[2,2,3,180]{3,2,1,0:T(4,128)S(1)}, f32[2,2,3,180]{3,2,1,0:T(4,128)S(1)}, u32[]{:S(2)}, u32[]{:S(2)}) collective-permute-start(f32[2,2,3,180]{3,2,1,0:T(4,128)S(1)} %pad_maximum_fusion.8), channel_id=1, source_target_pairs={{0,3},{1,0},{2,1},{3,2},{4,7},{5,4},{6,5},{7,6},{8,11},{9,8},{10,9... | collective-permute-start | bytes 25928 | tf_op jit(solution)/shard_map/ppermute | solution.py:163
  15.5 92.1 %all-gather.5.cloned.1.call-start = ((), (), s32[]{:S(2)}) async-start(), calls=%async_computation.7 | async-start | bytes 2826240 | tf_op jit(solution)/shard_map/all_gather | solution.py:250
  17.4 2.6 %copy-start.11 = (f32[2,180,96]{2,1,0:T(8,128)}, f32[2,180,96]{2,1,0:T(8,128)S(1)}, u32[]{:S(2)}) copy-start(f32[2,180,96]{2,1,0:T(8,128)S(1)} %pad_maximum_fusion.2) | copy-start | bytes 414724
  18.2 1.8 copy-start.2
  51.3 1.6 copy-start.17
  52.9 2.1 copy-start.6
  52.9 2.1 copy-start.18
  55.7 1.0 copy-start.1
  59.8 16.5 %copy-start.3 = (bf16[2,3,180,256]{3,0,2,1:T(2,128)(2,1)S(1)}, bf16[2,3,180,256]{3,0,2,1:T(2,128)(2,1)}, u32[]{:S(2)}) copy-start(bf16[2,3,180,256]{3,0,2,1:T(2,128)(2,1)} %param.8) | copy-start | bytes 1658884
  59.8 16.5 %copy-start.16 = (bf16[2,180,96]{2,1,0:T(8,128)(2,1)S(1)}, bf16[2,180,96]{2,1,0:T(8,128)(2,1)}, u32[]{:S(2)}) copy-start(bf16[2,180,96]{2,1,0:T(8,128)(2,1)} %pad_maximum_fusion.3) | copy-start | bytes 207364
  77.6 74.2 %reduce-scatter.5.cloned.1.call-start = ((), (), s32[]{:S(2)}) async-start(), calls=%async_computation.9 | async-start | bytes 2826240 | tf_op jit(solution)/shard_map/reduce_scatter | solution.py:194
  107.6 2.6 %copy-start.8 = (bf16[2,3,180,1024]{3,2,1,0:T(8,128)(2,1)S(1)}, bf16[2,3,180,1024]{3,2,1,0:T(8,128)(2,1)}, u32[]{:S(2)}) copy-start(bf16[2,3,180,1024]{3,2,1,0:T(8,128)(2,1)} %all-gather.5.cloned.1.call-done) | copy-start | bytes 6635524
  107.6 5.4 %slice-start = ((s8[4521984]{0:T(1024)(128)(4,1)}), s8[4194304]{0:T(1024)(128)(4,1)S(1)}, s32[]{:S(2)}) async-start(s8[4521984]{0:T(1024)(128)(4,1)} %bitcast.300), calls=%async_computation.10 | async-start | bytes 8388608
  110.2 2.9 %slice-start.1 = ((s8[4521984]{0:T(1024)(128)(4,1)}), s8[327680]{0:T(1024)(128)(4,1)S(1)}, s32[]{:S(2)}) async-start(s8[4521984]{0:T(1024)(128)(4,1)} %bitcast.300), calls=%async_computation.11 | async-start | bytes 655360
  113.0 5.4 %copy-start.19 = (f32[2,3,180,1024]{3,2,1,0:T(8,128)}, f32[2,3,180,1024]{3,2,1,0:T(8,128)S(1)}, u32[]{:S(2)}) copy-start(f32[2,3,180,1024]{3,2,1,0:T(8,128)S(1)} %fusion.14) | copy-start | bytes 13271044
  118.5 88.8 %reduce-scatter.3.cloned.1.call-start = ((), (), s32[]{:S(2)}) async-start(), calls=%async_computation.8 | async-start | bytes 2826240 | tf_op jit(solution)/shard_map/reduce_scatter | solution.py:194
  125.5 5.2 %collective-permute-start.4 = (f32[2,2,3,180]{3,2,1,0:T(4,128)S(1)}, f32[2,2,3,180]{3,2,1,0:T(4,128)S(1)}, u32[]{:S(2)}, u32[]{:S(2)}) collective-permute-start(f32[2,2,3,180]{3,2,1,0:T(4,128)S(1)} %pad_maximum_fusion.9), channel_id=1, source_target_pairs={{0,2},{1,3},{2,0},{3,1},{4,6},{5,7},{6,4},{7,5},{8,10},{9,11},{10,... | collective-permute-start | bytes 25928 | tf_op jit(solution)/shard_map/ppermute | solution.py:163
  128.0 4.0 %collective-permute-start.5 = (f32[2,2,3,180]{3,2,1,0:T(4,128)S(1)}, f32[2,2,3,180]{3,2,1,0:T(4,128)S(1)}, u32[]{:S(2)}, u32[]{:S(2)}) collective-permute-start(f32[2,2,3,180]{3,2,1,0:T(4,128)S(1)} %pad_maximum_fusion.9), channel_id=1, source_target_pairs={{0,1},{1,2},{2,3},{3,0},{4,5},{5,6},{6,7},{7,4},{8,9},{9,10},{10,1... | collective-permute-start | bytes 25928 | tf_op jit(solution)/shard_map/ppermute | solution.py:163
  128.0 4.0 %collective-permute-start.3 = (f32[2,2,3,180]{3,2,1,0:T(4,128)S(1)}, f32[2,2,3,180]{3,2,1,0:T(4,128)S(1)}, u32[]{:S(2)}, u32[]{:S(2)}) collective-permute-start(f32[2,2,3,180]{3,2,1,0:T(4,128)S(1)} %pad_maximum_fusion.9), channel_id=1, source_target_pairs={{0,3},{1,0},{2,1},{3,2},{4,7},{5,4},{6,5},{7,6},{8,11},{9,8},{10,9... | collective-permute-start | bytes 25928 | tf_op jit(solution)/shard_map/ppermute | solution.py:163
  178.5 2.1 copy-start.5
  180.9 1.0 copy-start.10
  182.3 17.0 %copy-start.13 = (bf16[2,3,180,256]{3,2,1,0:T(8,128)(2,1)S(1)}, bf16[2,3,180,256]{3,2,1,0:T(8,128)(2,1)}, u32[]{:S(2)}) copy-start(bf16[2,3,180,256]{3,2,1,0:T(8,128)(2,1)} %reduce-scatter.5.cloned.1.call-done) | copy-start | bytes 1658884
  183.0 16.4 %copy-start.4 = (bf16[2,3,180,256]{3,0,2,1:T(2,128)(2,1)S(1)}, bf16[2,3,180,256]{3,0,2,1:T(2,128)(2,1)}, u32[]{:S(2)}) copy-start(bf16[2,3,180,256]{3,0,2,1:T(2,128)(2,1)} %param.8) | copy-start | bytes 1658884
  183.0 16.4 %copy-start.7 = (bf16[2,3,180,256]{3,2,1,0:T(8,128)(2,1)S(1)}, bf16[2,3,180,256]{3,2,1,0:T(8,128)(2,1)}, u32[]{:S(2)}) copy-start(bf16[2,3,180,256]{3,2,1,0:T(8,128)(2,1)} %fusion.37) | copy-start | bytes 1658884
  183.0 16.4 %copy-start.9 = (bf16[2,3,180,256]{3,0,2,1:T(2,128)(2,1)S(1)}, bf16[2,3,180,256]{3,0,2,1:T(2,128)(2,1)}, u32[]{:S(2)}) copy-start(bf16[2,3,180,256]{3,0,2,1:T(2,128)(2,1)} %param.9) | copy-start | bytes 1658884
  183.0 16.4 %copy-start.12 = (f32[2,180,96]{2,1,0:T(8,128)S(1)}, f32[2,180,96]{2,1,0:T(8,128)}, u32[]{:S(2)}) copy-start(f32[2,180,96]{2,1,0:T(8,128)} %copy-done.11) | copy-start | bytes 414724
  202.1 4.2 %collective-permute-start.7 = (f32[2,2,3,180]{3,2,1,0:T(4,128)S(1)}, f32[2,2,3,180]{3,2,1,0:T(4,128)S(1)}, u32[]{:S(2)}, u32[]{:S(2)}) collective-permute-start(f32[2,2,3,180]{3,2,1,0:T(4,128)S(1)} %pad_maximum_fusion.10), channel_id=1, source_target_pairs={{0,2},{1,3},{2,0},{3,1},{4,6},{5,7},{6,4},{7,5},{8,10},{9,11},{10,... | collective-permute-start | bytes 25928 | tf_op jit(solution)/shard_map/ppermute | solution.py:163
  203.4 3.8 %collective-permute-start.8 = (f32[2,2,3,180]{3,2,1,0:T(4,128)S(1)}, f32[2,2,3,180]{3,2,1,0:T(4,128)S(1)}, u32[]{:S(2)}, u32[]{:S(2)}) collective-permute-start(f32[2,2,3,180]{3,2,1,0:T(4,128)S(1)} %pad_maximum_fusion.10), channel_id=1, source_target_pairs={{0,1},{1,2},{2,3},{3,0},{4,5},{5,6},{6,7},{7,4},{8,9},{9,10},{10,1... | collective-permute-start | bytes 25928 | tf_op jit(solution)/shard_map/ppermute | solution.py:163
  203.4 3.8 %collective-permute-start.6 = (f32[2,2,3,180]{3,2,1,0:T(4,128)S(1)}, f32[2,2,3,180]{3,2,1,0:T(4,128)S(1)}, u32[]{:S(2)}, u32[]{:S(2)}) collective-permute-start(f32[2,2,3,180]{3,2,1,0:T(4,128)S(1)} %pad_maximum_fusion.10), channel_id=1, source_target_pairs={{0,3},{1,0},{2,1},{3,2},{4,7},{5,4},{6,5},{7,6},{8,11},{9,8},{10,9... | collective-permute-start | bytes 25928 | tf_op jit(solution)/shard_map/ppermute | solution.py:163
Sparse Core Ops, SparseCore 0:
  15.6 35.1 all-gather.2
  77.7 29.8 all-gather.4
  118.6 33.1 reduce-scatter.4
  154.2 30.7 reduce-scatter.2
where the time goes:
time: 220 us
  blocking collectives  79.8 us (36%)
  waiting for transfers between devices  45.3 us (21%)
  matrix products  38.3 us (17%)
  starting transfers between devices  15.8 us (7%)
  between operations  14.4 us (7%)
  local copies, waits for them, and re-layouts  13.1 us (6%)
  other arithmetic  12.9 us (6%)
    all_to_all x2, blocking collectives, stacked_columns(): lax.all_to_all(field.astype(link_type), 'space', 3, 2, tiled=True)  47.9 us
    all_to_all x2, blocking collectives, stacked_rows(): lax.all_to_all(field.astype(link_type), 'space', 2, 3, tiled=True)  31.9 us
    all_gather x1, waiting for transfers between devices, per_device(): whole_residual = lax.all_gather(residual, 'feat', axis=3, tiled=True)  23 us
    reduce_scatter x2, waiting for transfers between devices, channel_share(): lax.psum_scatter(term.astype(jnp.bfloat16), 'feat', scatter_dimension=3,...  19.8 us
    ppermute x9, starting transfers between devices, token_sums(): lax.ppermute(pair, 'feat', [(i, (i + count - shift) % count) for i in ran...  15.6 us
    dot_general x1, matrix products, per_device(): jnp.einsum('brwd,hd->brwh', whole_cotangent, down_weight, preferred_eleme...  6.92 us
    dot_general x1, matrix products, per_device(): jnp.einsum('brwh,hd->brwd', activated, down_weight, preferred_element_typ...  6.91 us
    dot_general x1, matrix products, per_device(): jnp.einsum('brwh,dh->brwd', grad_hidden, up_weight, preferred_element_typ...  5.41 us
  transfers between devices with their start and end apart: 13, of which 5 were waited for; matrix products, arithmetic and copies ran while one was open for 19% of the time, Pallas kernels for 0%

commit v1 on v0

--- a/solution.py
+++ b/solution.py
@@ -247,7 +247,8 @@
     )
     residual = (filtered + normed + values).astype(jnp.bfloat16)
     residual_vals = residual.astype(jnp.float32)
-    whole_residual = lax.all_gather(residual, "feat", axis=3, tiled=True)
+    repeated = jnp.stack([residual] * lax.axis_size("feat"))
+    whole_residual = jnp.concatenate(lax.all_to_all(repeated, "feat", 0, 0), axis=3)
     grad_act = jnp.einsum(
         "brwd,hd->brwh", whole_cotangent, down_weight, preferred_element_type=jnp.float32
     )

time: 220 us -> 228 us (1.036)
  local copies, waits for them, and re-layouts: 13.1 us -> 25.1 us
  waiting for transfers between devices: 45.3 us -> 39.7 us
  starting transfers between devices: 15.8 us -> 18.3 us
    all_gather x1 -> x0, waiting for transfers between devices: 23 us -> none  [per_device(): whole_residual = lax.all_gather(residual, 'feat', axis=3, tiled=True)]
    all_to_all x0 -> x1, waiting for transfers between devices: none -> 21 us  [per_device(): lax.all_to_all(repeated, 'feat', 0, 0)]
    reshape x0 -> x2, local copies, waits for them, and re-layouts: none -> 8.17 us  [per_device(): jnp.concatenate(lax.all_to_all(repeated, 'feat', 0, 0), axis=3)]
    all_to_all x0 -> x1, starting transfers between devices: none -> 4.46 us  [per_device(): lax.all_to_all(repeated, 'feat', 0, 0)]
    reduce_scatter x2, waiting for transfers between devices: 19.8 us -> 15.5 us  [channel_share(): lax.psum_scatter(term.astype(jnp.bfloat16), 'feat', scatter_dimension=3,...]
    another operation x0 -> x1, local copies, waits for them, and re-layouts: none -> 2.48 us  [per_device(): repeated = jnp.stack([residual] * lax.axis_size('feat'))]
  transfers between devices with their start and end apart: 13 -> 13, of which waited for: 5 -> 6; matrix products, arithmetic and copies ran while one was open for 19% -> 18% of each run, Pallas kernels for 0% -> 0%
where the time goes in v1:
time: 228 us; the launch traced here: 227 us
  blocking collectives  79.4 us (35%)
  waiting for transfers between devices  39.7 us (17%)
  matrix products  37.5 us (16%)
  local copies, waits for them, and re-layouts  25.1 us (11%)
  starting transfers between devices  18.3 us (8%)
  between operations  14.4 us (6%)
  other arithmetic  13 us (6%)
    all_to_all x2, blocking collectives, stacked_columns(): lax.all_to_all(field.astype(link_type), 'space', 3, 2, tiled=True)  47.5 us
    all_to_all x2, blocking collectives, stacked_rows(): lax.all_to_all(field.astype(link_type), 'space', 2, 3, tiled=True)  31.9 us
    all_to_all x1, waiting for transfers between devices, per_device(): lax.all_to_all(repeated, 'feat', 0, 0)  21 us
    reduce_scatter x2, waiting for transfers between devices, channel_share(): lax.psum_scatter(term.astype(jnp.bfloat16), 'feat', scatter_dimension=3,...  15.5 us
    ppermute x9, starting transfers between devices, token_sums(): lax.ppermute(pair, 'feat', [(i, (i + count - shift) % count) for i in ran...  13.5 us
    reshape x2, local copies, waits for them, and re-layouts, per_device(): jnp.concatenate(lax.all_to_all(repeated, 'feat', 0, 0), axis=3)  8.17 us
    dot_general x1, matrix products, per_device(): jnp.einsum('brwd,hd->brwh', whole_cotangent, down_weight, preferred_eleme...  6.92 us
    dot_general x1, matrix products, per_device(): jnp.einsum('brwh,hd->brwd', activated, down_weight, preferred_element_typ...  6.91 us
  transfers between devices with their start and end apart: 13, of which 6 were waited for; matrix products, arithmetic and copies ran while one was open for 18% of the time, Pallas kernels for 0%

profile of v1, /device:TPU:1, one launch (start us, length us, event | category | flops | bytes accessed | tf_op | source)
XLA Modules:
  0.0 227.4 jit_solution(18382419430244936331)
XLA Ops:
  7.2 1.7 convert_reduce_fusion.1
  9.0 3.8 %collective-permute-start.1 = (f32[2,2,3,180]{3,2,1,0:T(4,128)S(1)}, f32[2,2,3,180]{3,2,1,0:T(4,128)S(1)}, u32[]{:S(2)}, u32[]{:S(2)}) collective-permute-start(f32[2,2,3,180]{3,2,1,0:T(4,128)S(1)} %pad_maximum_fusion.8), channel_id=1, source_target_pairs={{0,2},{1,3},{2,0},{3,1},{4,6},{5,7},{6,4},{7,5},{8,10},{9,11},{10,... | collective-permute-start | bytes 25928 | tf_op jit(solution)/shard_map/ppermute | solution.py:163
  13.2 2.3 %collective-permute-start = (f32[2,2,3,180]{3,2,1,0:T(4,128)S(1)}, f32[2,2,3,180]{3,2,1,0:T(4,128)S(1)}, u32[]{:S(2)}, u32[]{:S(2)}) collective-permute-start(f32[2,2,3,180]{3,2,1,0:T(4,128)S(1)} %pad_maximum_fusion.8), channel_id=1, source_target_pairs={{0,3},{1,0},{2,1},{3,2},{4,7},{5,4},{6,5},{7,6},{8,11},{9,8},{10,9... | collective-permute-start | bytes 25928 | tf_op jit(solution)/shard_map/ppermute | solution.py:163
  17.4 0.7 pad_maximum_fusion.1
  18.2 1.1 maximum_bitcast_fusion.1
  19.3 0.7 pad_maximum_fusion.3
  20.1 1.0 convolution_bitcast_fusion.7
  21.1 0.9 copy.97
  22.0 28.2 %all_to_all.77 = f32[2,2,3,96,256]{4,1,2,0,3:T(2,128)S(1)} all-to-all(f32[2,2,3,96,256]{4,1,2,0,3:T(2,128)S(1)} %copy.97), channel_id=1, replica_groups=mesh['space'=32,'feat'=4] {'space'}, dimensions={3} | all-to-all | bytes 2359296 | tf_op jit(solution)/shard_map/all_to_all | solution.py:150
  50.6 0.7 convolution_bitcast_fusion.6
  51.3 1.6 reshape.203
  52.9 2.1 fusion.31
  55.0 0.6 fusion.32
  55.7 1.0 copy-done.1
  56.8 1.0 copy_bitcast_fusion
  57.7 1.4 fusion.42
  59.1 0.6 copy.109
  59.8 16.0 %all_to_all.78 = bf16[2,2,96,3,256]{4,0,3,1,2:T(2,128)(2,1)S(1)} all-to-all(bf16[2,2,96,3,256]{4,0,3,1,2:T(2,128)(2,1)S(1)} %copy.109), channel_id=1, replica_groups=mesh['space'=32,'feat'=4] {'space'}, dimensions={2} | all-to-all | bytes 1179648 | tf_op jit(solution)/shard_map/all_to_all | solution.py:154
  76.8 0.9 copy-done.8
  78.1 2.5 %stack.151 = bf16[4,2,3,180,256]{4,1,3,2,0:T(2,128)(2,1)} broadcast(bf16[2,3,180,256]{3,0,2,1:T(2,128)(2,1)S(1)} %copy.113), dimensions={1,2,3,4} | broadcast | bytes 2764800 | tf_op jit(solution)/shard_map/stack | solution.py:250
  80.5 4.5 %all-to-all-start.2 = ((bf16[4,2,3,180,256]{4,1,3,2,0:T(2,128)(2,1)}), bf16[4,2,3,180,256]{4,1,3,2,0:T(2,128)(2,1)}, u32[]{:S(2)}, u32[]{:S(2)}) async-start(bf16[4,2,3,180,256]{4,1,3,2,0:T(2,128)(2,1)} %stack.151), calls=%async_computation.2 | async-start | bytes 4423680 | tf_op jit(solution)/shard_map/all_to_all | solution.py:251
  85.1 6.9 %fusion.16 = f32[2,3,180,1024]{3,2,1,0:T(8,128)} fusion(bf16[2,3,180,1024]{3,0,2,1:T(2,128)(2,1)} %all-gather.2.cloned.1.call-done, bf16[1024,1024]{1,0:T(8,128)(2,1)} %param.15), kind=kOutput, calls=%fused_computation.20 | convolution fusion | flops 2264924160 | bytes 8732672 | tf_op jit(solution)/shard_map/brwd,hd->brwh/dot_general | solution.py:252
  92.0 21.0 %all-to-all-done.2 = bf16[4,2,3,180,256]{4,1,3,2,0:T(2,128)(2,1)} async-done(((bf16[4,2,3,180,256]{4,1,3,2,0:T(2,128)(2,1)}), bf16[4,2,3,180,256]{4,1,3,2,0:T(2,128)(2,1)}, u32[]{:S(2)}, u32[]{:S(2)}) %all-to-all-start.2) | async-done | bytes 2211872 | tf_op jit(solution)/shard_map/all_to_all | solution.py:251
  112.9 3.8 %copy.114 = bf16[2,3,180,4,256]{4,3,2,1,0:T(4,128)(2,1)} copy(bf16[2,3,180,4,256]{4,0,2,1,3:T(2,128)(2,1)} %bitcast.59) | data formatting | bytes 4423680 | tf_op jit(solution)/shard_map/reshape | solution.py:251
  116.8 4.4 %reshape.206 = bf16[2,3,180,1024]{3,2,1,0:T(8,128)(2,1)} reshape(bf16[2,3,180,4,256]{4,3,2,1,0:T(4,128)(2,1)} %copy.114) | data formatting | bytes 4423680 | tf_op jit(solution)/shard_map/reshape | solution.py:251
  121.1 2.5 %convert_reduce_fusion = (f32[2,3,180]{2,1,0:T(4,128)S(1)}, f32[2,3,180]{2,1,0:T(4,128)S(1)}) fusion(bf16[2,3,180,1024]{3,2,1,0:T(8,128)(2,1)} %reshape.206), kind=kLoop, calls=%fused_computation.3 | loop fusion | flops 4421520 | bytes 2220480 | tf_op jit(solution)/shard_map/reduce_sum | solution.py:257
  123.7 2.8 %fusion.14 = f32[2,3,180,1024]{3,2,1,0:T(8,128)S(1)} fusion(bf16[2,3,180,1024]{3,2,1,0:T(8,128)(2,1)S(1)} %copy-done.2, f32[2,3,180]{2,1,0:T(4,128)S(1)} %get-tuple-element.60, f32[2,3,180]{2,1,0:T(4,128)S(1)} %get-tuple-element.59, bf16[1024,1024]{1,0:T(8,128)(2,1)S(1)} %copy-done), kind=kOutput, calls=%fused_computation.19 | convolution fusion | flops 2269347840 | bytes 8741312 | tf_op jit(solution)/shard_map/brwd,dh->brwh/dot_general | solution.py:261
  126.6 5.4 %fusion.123 = (f32[2,3,180]{2,1,0:T(4,128)S(1)}, f32[2,3,180]{2,1,0:T(4,128)S(1)}, bf16[2,3,180,1024]{3,2,1,0:T(8,128)(2,1)}) fusion(f32[2,3,180]{2,1,0:T(4,128)S(1)} %get-tuple-element.60, f32[2,3,180]{2,1,0:T(4,128)S(1)} %get-tuple-element.59, bf16[2,3,180,1024]{3,2,1,0:T(8,128)(2,1)S(1)} %copy-done.2, bf16[1024,1024]{1,0:T(8,128)(2,1)S(1)} %copy-done, ...), kind=kOutput, calls=%fused_computation.189 | convolution fusion | flops 2283722752 | bytes 15385472 | tf_op jit(solution)/shard_map/brwh,dh->brwd/dot_general | solution.py:270
  132.3 6.9 %fusion.28 = bf16[2,3,180,1024]{3,2,1,0:T(8,128)(2,1)} fusion(bf16[1024,1024]{1,0:T(8,128)(2,1)} %param.15, f32[2,3,180,1024]{3,2,1,0:T(8,128)} %copy-done.20), kind=kOutput, calls=%fused_computation.36 | convolution fusion | flops 2271559680 | bytes 8732672 | tf_op jit(solution)/shard_map/brwh,hd->brwd/dot_general | solution.py:265
  139.5 1.3 collective-permute-start.5
  140.8 1.4 collective-permute-start.3
  142.2 1.6 collective-permute-done.4
  144.3 15.5 %reduce-scatter.5.cloned.1.call-done = bf16[2,3,180,256]{3,2,1,0:T(8,128)(2,1)} async-done(((bf16[2,3,180,1024]{3,2,1,0:T(8,128)(2,1)}), bf16[2,3,180,256]{3,2,1,0:T(8,128)(2,1)}) %reduce-scatter.5.cloned.1.call-update) | async-done | bytes 552976 | tf_op jit(solution)/shard_map/reduce_scatter | solution.py:194
  159.8 2.3 %fusion.40 = bf16[2,2,3,96,256]{4,3,2,1,0:T(8,128)(2,1)S(1)} fusion(bf16[2,180,96]{2,1,0:T(8,128)(2,1)} %pad_maximum_fusion.3, bf16[2,3,180,256]{3,2,1,0:T(8,128)(2,1)} %copy-done.8, bf16[2,3,180,256]{3,2,1,0:T(8,128)(2,1)} %reduce-scatter.5.cloned.1.call-done, bf16[2,3,180,256]{3,0,2,1:T(2,128)(2,1)} %param.9, f32[2,3,180]{2,1,0:T(4,128)S(1)} %get-tuple-element.58, ...), kind=kOutput, calls=%fused_computation.61 | convolution fusion | flops 108933120 | bytes 2335104 | tf_op jit(solution)/shard_map/brwc,pwk->pbrkc/dot_general | solution.py:130
  162.1 0.6 copy.117
  162.7 19.3 %all_to_all.79 = bf16[2,2,3,96,256]{4,1,2,0,3:T(2,128)(2,1)S(1)} all-to-all(bf16[2,2,3,96,256]{4,1,2,0,3:T(2,128)(2,1)S(1)} %copy.117), channel_id=1, replica_groups=mesh['space'=32,'feat'=4] {'space'}, dimensions={3} | all-to-all | bytes 1179648 | tf_op jit(solution)/shard_map/all_to_all | solution.py:150
  182.5 1.2 convolution_bitcast_fusion.8
  183.7 2.5 %reshape.239 = bf16[2,2,96,3,2,128]{5,4,2,0,3,1:T(2,128)(2,1)} reshape(bf16[2,2,96,3,256]{4,2,0,3,1:T(8,128)(2,1)} %convolution_bitcast_fusion.8) | data formatting | bytes 1179648 | tf_op jit(solution)/shard_map/reshape | solution.py:60
  186.2 2.1 fusion.39
  188.6 0.6 copy.192
  190.6 15.9 %all_to_all.80 = bf16[2,2,96,3,256]{4,0,3,1,2:T(2,128)(2,1)S(1)} all-to-all(bf16[2,2,96,3,256]{4,0,3,1,2:T(2,128)(2,1)S(1)} %copy.129), channel_id=1, replica_groups=mesh['space'=32,'feat'=4] {'space'}, dimensions={2} | all-to-all | bytes 1179648 | tf_op jit(solution)/shard_map/all_to_all | solution.py:154
  207.0 2.7 %fusion.124 = (f32[2,3,180]{2,1,0:T(4,128)S(1)}, f32[2,3,180]{2,1,0:T(4,128)S(1)}, f32[2,3,180,256]{3,2,1,0:T(8,128)}) fusion(f32[2,3,180]{2,1,0:T(4,128)S(1)} %fusion.115, f32[2,3,180]{2,1,0:T(4,128)S(1)} %fusion.116, bf16[2,3,180,256]{3,0,2,1:T(2,128)(2,1)S(1)} %copy-done.5, bf16[2,2,3,96,256]{4,1,3,2,0:T(2,128)(2,1)S(1)} %bitcast.285, ...), kind=kOutput, calls=%fused_computation.190 | convolution fusion | flops 110866320 | bytes 4080384 | tf_op jit(solution)/shard_map/pbrkc,pwk->brwc/dot_general | solution.py:134
  209.7 1.4 collective-permute-start.7
  211.2 2.7 %collective-permute-start.6 = (f32[2,2,3,180]{3,2,1,0:T(4,128)S(1)}, f32[2,2,3,180]{3,2,1,0:T(4,128)S(1)}, u32[]{:S(2)}, u32[]{:S(2)}) collective-permute-start(f32[2,2,3,180]{3,2,1,0:T(4,128)S(1)} %pad_maximum_fusion.10), channel_id=1, source_target_pairs={{0,3},{1,0},{2,1},{3,2},{4,7},{5,4},{6,5},{7,6},{8,11},{9,8},{10,9... | collective-permute-start | bytes 25928 | tf_op jit(solution)/shard_map/ppermute | solution.py:163
  213.9 1.1 collective-permute-done.8
  215.0 3.4 %fusion.68 = (bf16[2,3,180,256]{3,2,1,0:T(8,128)(2,1)S(1)}, bf16[2,3,180,256]{3,2,1,0:T(8,128)(2,1)S(1)}) fusion(f32[2,3,180,256]{3,2,1,0:T(8,128)} %get-tuple-element.64, f32[2,3,180]{2,1,0:T(4,128)S(1)} %get-tuple-element.56, f32[2,3,180]{2,1,0:T(4,128)S(1)} %get-tuple-element.55, f32[2,3,180]{2,1,0:T(4,128)S(1)} %fusion.115, ...), kind=kLoop, calls=%fused_computation.92 | loop fusion | flops 6082560 | bytes 5011200 | tf_op jit(solution)/shard_map/convert_element_type | solution.py:306
  218.4 1.2 copy.134
  219.6 1.2 copy.133
  (100 shorter events, 8.0 us)
Async XLA Ops:
  7.2 116.5 %copy-start = (bf16[1024,1024]{1,0:T(8,128)(2,1)S(1)}, bf16[1024,1024]{1,0:T(8,128)(2,1)}, u32[]{:S(2)}) copy-start(bf16[1024,1024]{1,0:T(8,128)(2,1)} %param.14) | copy-start | bytes 6291460
  7.2 10.0 %copy-start.15 = (f32[2,2,128,128]{3,2,1,0:T(8,128)S(1)}, f32[2,2,128,128]{3,2,1,0:T(8,128)}, u32[]{:S(2)}) copy-start(f32[2,2,128,128]{3,2,1,0:T(8,128)} %param.10) | copy-start | bytes 786436
  7.2 50.5 %all-gather.2.cloned.1.call-start = ((), (), s32[]{:S(2)}) async-start(), calls=%async_computation.7 | async-start | bytes 2764800 | tf_op jit(solution)/shard_map/all_gather | solution.py:227
  9.0 8.3 %copy-start.16 = (f32[2,2,128,128]{3,2,1,0:T(8,128)S(1)}, f32[2,2,128,128]{3,2,1,0:T(8,128)}, u32[]{:S(2)}) copy-start(f32[2,2,128,128]{3,2,1,0:T(8,128)} %param.12) | copy-start | bytes 786436
  9.0 11.0 %collective-permute-start.1 = (f32[2,2,3,180]{3,2,1,0:T(4,128)S(1)}, f32[2,2,3,180]{3,2,1,0:T(4,128)S(1)}, u32[]{:S(2)}, u32[]{:S(2)}) collective-permute-start(f32[2,2,3,180]{3,2,1,0:T(4,128)S(1)} %pad_maximum_fusion.8), channel_id=1, source_target_pairs={{0,2},{1,3},{2,0},{3,1},{4,6},{5,7},{6,4},{7,5},{8,10},{9,11},{10,... | collective-permute-start | bytes 25928 | tf_op jit(solution)/shard_map/ppermute | solution.py:163
  12.8 7.2 %collective-permute-start.2 = (f32[2,2,3,180]{3,2,1,0:T(4,128)S(1)}, f32[2,2,3,180]{3,2,1,0:T(4,128)S(1)}, u32[]{:S(2)}, u32[]{:S(2)}) collective-permute-start(f32[2,2,3,180]{3,2,1,0:T(4,128)S(1)} %pad_maximum_fusion.8), channel_id=1, source_target_pairs={{0,1},{1,2},{2,3},{3,0},{4,5},{5,6},{6,7},{7,4},{8,9},{9,10},{10,1... | collective-permute-start | bytes 25928 | tf_op jit(solution)/shard_map/ppermute | solution.py:163
  13.2 6.8 %collective-permute-start = (f32[2,2,3,180]{3,2,1,0:T(4,128)S(1)}, f32[2,2,3,180]{3,2,1,0:T(4,128)S(1)}, u32[]{:S(2)}, u32[]{:S(2)}) collective-permute-start(f32[2,2,3,180]{3,2,1,0:T(4,128)S(1)} %pad_maximum_fusion.8), channel_id=1, source_target_pairs={{0,3},{1,0},{2,1},{3,2},{4,7},{5,4},{6,5},{7,6},{8,11},{9,8},{10,9... | collective-permute-start | bytes 25928 | tf_op jit(solution)/shard_map/ppermute | solution.py:163
  17.4 2.7 %copy-start.12 = (f32[2,180,96]{2,1,0:T(8,128)}, f32[2,180,96]{2,1,0:T(8,128)S(1)}, u32[]{:S(2)}) copy-start(f32[2,180,96]{2,1,0:T(8,128)S(1)} %pad_maximum_fusion.2) | copy-start | bytes 414724
  18.2 1.8 copy-start.3
  51.3 1.6 copy-start.18
  52.9 2.1 copy-start.7
  52.9 2.1 copy-start.19
  55.7 1.1 copy-start.1
  59.8 16.5 %copy-start.4 = (bf16[2,3,180,256]{3,0,2,1:T(2,128)(2,1)S(1)}, bf16[2,3,180,256]{3,0,2,1:T(2,128)(2,1)}, u32[]{:S(2)}) copy-start(bf16[2,3,180,256]{3,0,2,1:T(2,128)(2,1)} %param.8) | copy-start | bytes 1658884
  59.8 16.5 %copy-start.17 = (bf16[2,180,96]{2,1,0:T(8,128)(2,1)S(1)}, bf16[2,180,96]{2,1,0:T(8,128)(2,1)}, u32[]{:S(2)}) copy-start(bf16[2,180,96]{2,1,0:T(8,128)(2,1)} %pad_maximum_fusion.3) | copy-start | bytes 207364
  76.7 0.9 copy-start.8
  80.5 32.4 %all-to-all-start.2 = ((bf16[4,2,3,180,256]{4,1,3,2,0:T(2,128)(2,1)}), bf16[4,2,3,180,256]{4,1,3,2,0:T(2,128)(2,1)}, u32[]{:S(2)}, u32[]{:S(2)}) async-start(bf16[4,2,3,180,256]{4,1,3,2,0:T(2,128)(2,1)} %stack.151), calls=%async_computation.2 | async-start | bytes 4423680 | tf_op jit(solution)/shard_map/all_to_all | solution.py:251
  85.0 74.8 %reduce-scatter.5.cloned.1.call-start = ((), (), s32[]{:S(2)}) async-start(), calls=%async_computation.9 | async-start | bytes 2826240 | tf_op jit(solution)/shard_map/reduce_scatter | solution.py:194
  121.1 2.6 %copy-start.2 = (bf16[2,3,180,1024]{3,2,1,0:T(8,128)(2,1)S(1)}, bf16[2,3,180,1024]{3,2,1,0:T(8,128)(2,1)}, u32[]{:S(2)}) copy-start(bf16[2,3,180,1024]{3,2,1,0:T(8,128)(2,1)} %reshape.206) | copy-start | bytes 6635524
  121.1 5.4 %slice-start = ((s8[4521984]{0:T(1024)(128)(4,1)}), s8[4194304]{0:T(1024)(128)(4,1)S(1)}, s32[]{:S(2)}) async-start(s8[4521984]{0:T(1024)(128)(4,1)} %bitcast.301), calls=%async_computation.10 | async-start | bytes 8388608
  123.7 2.9 %slice-start.1 = ((s8[4521984]{0:T(1024)(128)(4,1)}), s8[327680]{0:T(1024)(128)(4,1)S(1)}, s32[]{:S(2)}) async-start(s8[4521984]{0:T(1024)(128)(4,1)} %bitcast.301), calls=%async_computation.11 | async-start | bytes 655360
  126.6 5.4 %copy-start.20 = (f32[2,3,180,1024]{3,2,1,0:T(8,128)}, f32[2,3,180,1024]{3,2,1,0:T(8,128)S(1)}, u32[]{:S(2)}) copy-start(f32[2,3,180,1024]{3,2,1,0:T(8,128)S(1)} %fusion.14) | copy-start | bytes 13271044
  132.1 83.0 %reduce-scatter.3.cloned.1.call-start = ((), (), s32[]{:S(2)}) async-start(), calls=%async_computation.8 | async-start | bytes 2826240 | tf_op jit(solution)/shard_map/reduce_scatter | solution.py:194
  139.3 4.5 %collective-permute-start.4 = (f32[2,2,3,180]{3,2,1,0:T(4,128)S(1)}, f32[2,2,3,180]{3,2,1,0:T(4,128)S(1)}, u32[]{:S(2)}, u32[]{:S(2)}) collective-permute-start(f32[2,2,3,180]{3,2,1,0:T(4,128)S(1)} %pad_maximum_fusion.9), channel_id=1, source_target_pairs={{0,2},{1,3},{2,0},{3,1},{4,6},{5,7},{6,4},{7,5},{8,10},{9,11},{10,... | collective-permute-start | bytes 25928 | tf_op jit(solution)/shard_map/ppermute | solution.py:163
  139.5 4.7 %collective-permute-start.5 = (f32[2,2,3,180]{3,2,1,0:T(4,128)S(1)}, f32[2,2,3,180]{3,2,1,0:T(4,128)S(1)}, u32[]{:S(2)}, u32[]{:S(2)}) collective-permute-start(f32[2,2,3,180]{3,2,1,0:T(4,128)S(1)} %pad_maximum_fusion.9), channel_id=1, source_target_pairs={{0,1},{1,2},{2,3},{3,0},{4,5},{5,6},{6,7},{7,4},{8,9},{9,10},{10,1... | collective-permute-start | bytes 25928 | tf_op jit(solution)/shard_map/ppermute | solution.py:163
  140.8 3.4 %collective-permute-start.3 = (f32[2,2,3,180]{3,2,1,0:T(4,128)S(1)}, f32[2,2,3,180]{3,2,1,0:T(4,128)S(1)}, u32[]{:S(2)}, u32[]{:S(2)}) collective-permute-start(f32[2,2,3,180]{3,2,1,0:T(4,128)S(1)} %pad_maximum_fusion.9), channel_id=1, source_target_pairs={{0,3},{1,0},{2,1},{3,2},{4,7},{5,4},{6,5},{7,6},{8,11},{9,8},{10,9... | collective-permute-start | bytes 25928 | tf_op jit(solution)/shard_map/ppermute | solution.py:163
  186.2 2.1 copy-start.6
  188.6 1.0 copy-start.11
  190.0 17.0 %copy-start.14 = (bf16[2,3,180,256]{3,2,1,0:T(8,128)(2,1)S(1)}, bf16[2,3,180,256]{3,2,1,0:T(8,128)(2,1)}, u32[]{:S(2)}) copy-start(bf16[2,3,180,256]{3,2,1,0:T(8,128)(2,1)} %reduce-scatter.5.cloned.1.call-done) | copy-start | bytes 1658884
  190.6 16.4 %copy-start.5 = (bf16[2,3,180,256]{3,0,2,1:T(2,128)(2,1)S(1)}, bf16[2,3,180,256]{3,0,2,1:T(2,128)(2,1)}, u32[]{:S(2)}) copy-start(bf16[2,3,180,256]{3,0,2,1:T(2,128)(2,1)} %param.8) | copy-start | bytes 1658884
  190.6 16.4 %copy-start.9 = (bf16[2,3,180,256]{3,2,1,0:T(8,128)(2,1)S(1)}, bf16[2,3,180,256]{3,2,1,0:T(8,128)(2,1)}, u32[]{:S(2)}) copy-start(bf16[2,3,180,256]{3,2,1,0:T(8,128)(2,1)} %copy-done.8) | copy-start | bytes 1658884
  190.6 16.4 %copy-start.10 = (bf16[2,3,180,256]{3,0,2,1:T(2,128)(2,1)S(1)}, bf16[2,3,180,256]{3,0,2,1:T(2,128)(2,1)}, u32[]{:S(2)}) copy-start(bf16[2,3,180,256]{3,0,2,1:T(2,128)(2,1)} %param.9) | copy-start | bytes 1658884
  190.6 16.4 %copy-start.13 = (f32[2,180,96]{2,1,0:T(8,128)S(1)}, f32[2,180,96]{2,1,0:T(8,128)}, u32[]{:S(2)}) copy-start(f32[2,180,96]{2,1,0:T(8,128)} %copy-done.12) | copy-start | bytes 414724
  209.7 4.2 %collective-permute-start.7 = (f32[2,2,3,180]{3,2,1,0:T(4,128)S(1)}, f32[2,2,3,180]{3,2,1,0:T(4,128)S(1)}, u32[]{:S(2)}, u32[]{:S(2)}) collective-permute-start(f32[2,2,3,180]{3,2,1,0:T(4,128)S(1)} %pad_maximum_fusion.10), channel_id=1, source_target_pairs={{0,2},{1,3},{2,0},{3,1},{4,6},{5,7},{6,4},{7,5},{8,10},{9,11},{10,... | collective-permute-start | bytes 25928 | tf_op jit(solution)/shard_map/ppermute | solution.py:163
  211.2 3.8 %collective-permute-start.8 = (f32[2,2,3,180]{3,2,1,0:T(4,128)S(1)}, f32[2,2,3,180]{3,2,1,0:T(4,128)S(1)}, u32[]{:S(2)}, u32[]{:S(2)}) collective-permute-start(f32[2,2,3,180]{3,2,1,0:T(4,128)S(1)} %pad_maximum_fusion.10), channel_id=1, source_target_pairs={{0,1},{1,2},{2,3},{3,0},{4,5},{5,6},{6,7},{7,4},{8,9},{9,10},{10,1... | collective-permute-start | bytes 25928 | tf_op jit(solution)/shard_map/ppermute | solution.py:163
  211.2 3.8 %collective-permute-start.6 = (f32[2,2,3,180]{3,2,1,0:T(4,128)S(1)}, f32[2,2,3,180]{3,2,1,0:T(4,128)S(1)}, u32[]{:S(2)}, u32[]{:S(2)}) collective-permute-start(f32[2,2,3,180]{3,2,1,0:T(4,128)S(1)} %pad_maximum_fusion.10), channel_id=1, source_target_pairs={{0,3},{1,0},{2,1},{3,2},{4,7},{5,4},{6,5},{7,6},{8,11},{9,8},{10,9... | collective-permute-start | bytes 25928 | tf_op jit(solution)/shard_map/ppermute | solution.py:163
Sparse Core Ops, SparseCore 0:
  15.6 35.1 all-gather.1
  132.2 27.5 reduce-scatter.4
  162.3 30.5 reduce-scatter.2
